TPU v7x, 256 devices: a whole 4x4x8 slice. The times are simulated.
256 devices in a mesh: grp: 8 (over x_hi, y), dev: 32 (over z, x_lo, core).
Axes of the slice: x: 4 (x_hi: 2, x_lo: 2; x = x_hi * 2 + x_lo), y: 4, z: 8, core: 2. Of those that a mesh axis runs over, the one named last changes fastest.
Arguments:
- slab: bfloat16 [16, 8000, 8000], P('grp', 'dev'), may hold values from -2.5 to 2.5
- orbitals: bfloat16 [8000, 640], P('dev'), may hold values from -0.0625 to 0.0625
- hcore: float32 [8000, 8000], P('dev', 'grp'), may hold values from -6 to 6
- metric_inv: float32 [16, 16], replicated, may hold values from -1 to 2, as said below
Outputs:
- fock: float32 [8000, 8000], P('dev', 'grp')
Inputs may be any that keep to these rules, and one draw needn't show every extreme that they name: `metric_inv`: symmetric.
All inputs are finite; a program needn't handle non-finite values.
Results may differ from a plain program's by a relative error of at most 0.0065.
Values may be sent and summed in bfloat16 or wider, within the bound.
No kernel may reach another device: no remote copies, remote signals or barrier semaphores. Data moves between devices by JAX's collectives and lax.ppermute only.
A program may use at most 192 MiB of HBM per device.

v0:
```python
import jax
import jax.numpy as jnp
from jax import lax
from jax.sharding import PartitionSpec as P


def shards(slab, orbitals, hcore, metric_inv):
    aux_count = slab.shape[0]
    row_count = slab.shape[1]
    full_width = slab.shape[2]
    occ_count = orbitals.shape[1]
    slab_flat = slab.reshape(aux_count * row_count, full_width)
    half_done = jnp.dot(
        slab_flat,
        lax.all_gather(orbitals, "dev", axis=0, tiled=True),
        preferred_element_type=jnp.float32,
    )
    half_done = half_done.astype(jnp.bfloat16).reshape(aux_count, row_count, occ_count)
    aux_density = jnp.sum(
        half_done.astype(jnp.float32) * orbitals.astype(jnp.float32)[None], axis=(1, 2)
    )
    group_index = lax.axis_index("grp")
    group_density = lax.psum(aux_density, "dev")
    density_all = lax.all_gather(group_density, "grp", axis=0, tiled=True)
    fit_coef = jnp.dot(metric_inv, density_all, precision=lax.Precision.HIGHEST)
    half_flat = jnp.transpose(half_done, (1, 0, 2)).reshape(row_count, aux_count * occ_count)
    exchange_part = lax.dot_general(
        half_flat,
        lax.all_gather(half_flat, "dev", axis=0, tiled=True),
        (((1,), (1,)), ((), ())),
        preferred_element_type=jnp.float32,
    )
    local_coef = lax.dynamic_slice_in_dim(fit_coef, group_index * aux_count, aux_count)
    coulomb_part = jnp.zeros((row_count, full_width), jnp.float32)
    for aux_index in range(aux_count):
        coulomb_part = coulomb_part + local_coef[aux_index] * slab[aux_index].astype(jnp.float32)
    reduced = lax.psum_scatter(
        2.0 * coulomb_part - exchange_part, "grp", scatter_dimension=1, tiled=True
    )
    fock = hcore + reduced
    return fock


def solution(mesh):
    return jax.shard_map(
        shards,
        mesh=mesh,
        in_specs=(P("grp", "dev", None), P("dev", None), P("dev", "grp"), P()),
        out_specs=P("dev", "grp"),
        check_vma=False,
    )
```

profile of v0, /device:TPU:1, one launch (start us, length us, event | category | flops | bytes accessed | tf_op | source)
XLA Modules:
  0.0 403.7 jit_solution(6335460769524792547)
XLA Ops:
  6.5 0.7 all-gather.5.cloned.1.call-update
  7.3 0.0 all-gather.7.cloned.1.call-start
  7.3 1.1 mul.37
  8.4 0.1 mul.38
  8.5 7.4 %copy.19 = bf16[2,250,8000]{2,1,0:T(8,128)(2,1)} copy(bf16[2,250,8000]{2,0,1:T(2,128)(2,1)} %param.4) | data formatting | bytes 16000000 | tf_op args[0]
  15.9 10.1 %reshape.21 = bf16[500,8000]{1,0:T(8,128)(2,1)} reshape(bf16[2,250,8000]{2,1,0:T(8,128)(2,1)} %copy.19) | data formatting | bytes 16000000 | tf_op jit(solution)/shard_map/reshape | solution.py:12
  25.9 61.7 %all-gather.5.cloned.1.call-done = bf16[32,250,640]{2,1,0:T(8,128)(2,1)} async-done(((bf16[1,250,640]{2,1,0:T(8,128)(2,1)}), bf16[32,250,640]{2,1,0:T(8,128)(2,1)}) %all-gather.5.cloned.1.call-update) | async-done | bytes 10240016 | tf_op jit(solution)/shard_map/all_gather | solution.py:15
  87.6 10.9 %reshape.28 = bf16[8000,640]{1,0:T(8,128)(2,1)} reshape(bf16[32,250,640]{2,1,0:T(8,128)(2,1)} %all-gather.5.cloned.1.call-done) | data formatting | bytes 20480000
  98.5 12.2 %multiply_reduce_fusion = (f32[500]{0:T(512)S(1)}, bf16[500,640]{1,0:T(8,128)(2,1)S(1)}) fusion(f32[500,640]{1,0:T(8,128)S(1)} %mul.38, bf16[500,8000]{1,0:T(8,128)(2,1)} %reshape.21, bf16[8000,640]{1,0:T(8,128)(2,1)} %reshape.28), kind=kOutput, calls=%fused_computation.2 | convolution fusion | flops 5121279488 | bytes 20162000 | tf_op jit(solution)/shard_map/dot_general | solution.py:13
  110.8 0.1 reshape.22
  110.9 0.3 copy.22
  111.2 1.1 copy.24
  112.2 0.0 all-gather.7.cloned.1.call-update
  112.3 0.0 reduce-scatter.2.cloned.1.call-start
  112.3 17.1 %fusion.1 = (bf16[1,250,8000]{2,0,1:T(2,128)(2,1)}, bf16[1,250,8000]{2,0,1:T(2,128)(2,1)}) fusion(bf16[2,250,8000]{2,0,1:T(2,128)(2,1)} %param.4), kind=kLoop, calls=%fused_computation.5 | loop fusion | bytes 16000000 | tf_op jit(solution)/shard_map/slice | solution.py:36
  129.5 17.3 %copy.25 = bf16[1,250,8000]{1,2,0:T(8,128)(2,1)} copy(bf16[1,250,8000]{2,0,1:T(2,128)(2,1)} %get-tuple-element.5) | data formatting | bytes 8000000
  146.8 17.4 %copy.26 = bf16[1,250,8000]{1,2,0:T(8,128)(2,1)} copy(bf16[1,250,8000]{2,0,1:T(2,128)(2,1)} %get-tuple-element.6) | data formatting | bytes 8000000
  164.1 0.6 dynamic-slice.1
  164.7 0.1 reduce_sum.14
  164.8 0.1 reduce_sum.18
  165.5 54.1 %psum.7 = f32[2]{0:T(128)S(1)} all-reduce(f32[2]{0:T(128)S(1)} %reduce_sum.18), channel_id=1, replica_groups=mesh['grp'=8,'dev'=32] {'dev'}, use_global_device_ids=true, to_apply=%region_2.0 | all-reduce | flops 2 | bytes 16 | tf_op jit(solution)/shard_map/psum | solution.py:23
  219.7 0.2 dynamic-update-slice
  219.9 20.7 %all-reduce = f32[16]{0:T(128)S(1)} all-reduce(f32[16]{0:T(128)S(1)} %dynamic-update-slice), channel_id=1, replica_groups=mesh['grp'=8,'dev'=32] {'grp'}, use_global_device_ids=true, to_apply=%add | all-reduce | flops 16 | bytes 128
  240.6 0.0 copy-done
  240.6 0.1 convolution_bitcast_fusion
  240.7 0.1 dynamic_slice.3
  240.8 0.6 fusion.2
  241.4 17.5 %reshape.30 = bf16[8000,1280]{1,0:T(8,128)(2,1)} reshape(bf16[32,250,1280]{2,1,0:T(8,128)(2,1)} %all-gather.7.cloned.1.call-done) | data formatting | bytes 40960000
  258.9 15.5 %convolution_subtract_fusion = f32[250,8000]{0,1:T(8,128)} fusion(bf16[250,1280]{0,1:T(8,128)(2,1)S(1)} %bitcast.20, bf16[8000,1280]{1,0:T(8,128)(2,1)} %reshape.30, bf16[1,250,8000]{1,2,0:T(8,128)(2,1)} %copy.26, bf16[1,250,8000]{1,2,0:T(8,128)(2,1)} %copy.25, f32[]{:T(128)} %bitcast.5, f32[]{:T(128)} %bitcast.4), kind=kOutput, calls=%fused_computation | convolution fusion | flops 5134000128 | bytes 37120008 | tf_op jit(solution)/shard_map/dot_general | solution.py:27
  274.4 0.0 reduce-scatter.2.cloned.1.call-update
  274.4 120.3 %reduce-scatter.2.cloned.1.call-done = f32[250,1000]{0,1:T(8,128)} async-done(((f32[250,8000]{0,1:T(8,128)}), f32[250,1000]{0,1:T(8,128)}) %reduce-scatter.2.cloned.1.call-update) | async-done | bytes 1000016 | tf_op jit(solution)/shard_map/reduce_scatter | solution.py:37
  394.8 2.4 add.16
  (8 shorter events, 0.0 us)
Async XLA Ops:
  6.5 234.0 %copy-start = (f32[16,16]{1,0:T(8,128)S(1)}, f32[16,16]{1,0:T(8,128)}, u32[]{:S(2)}) copy-start(f32[16,16]{1,0:T(8,128)} %param.7) | copy-start | bytes 3076
  6.5 81.1 %all-gather.5.cloned.1.call-start = ((), (), s32[]{:S(2)}) async-start(), calls=%async_computation.2 | async-start | bytes 10813440 | tf_op jit(solution)/shard_map/all_gather | solution.py:15
  7.3 234.1 %all-gather.7.cloned.1.call-start = ((), (), s32[]{:S(2)}) async-start(), calls=%async_computation.3 | async-start | bytes 21626880 | tf_op jit(solution)/shard_map/all_gather | solution.py:29
  112.3 282.5 %reduce-scatter.2.cloned.1.call-start = ((), (), s32[]{:S(2)}) async-start(), calls=%async_computation.1 | async-start | bytes 9216000 | tf_op jit(solution)/shard_map/reduce_scatter | solution.py:37
  146.8 17.4 %copy-start.2 = (u32[256]{0:T(256)S(1)}, u32[256]{0:T(256)}, u32[]{:S(2)}) copy-start(u32[256]{0:T(256)} %constant.21) | copy-start | bytes 3076
  274.4 120.4 %copy-start.1 = (f32[250,1000]{0,1:T(8,128)S(1)}, f32[250,1000]{0,1:T(8,128)}, u32[]{:S(2)}) copy-start(f32[250,1000]{0,1:T(8,128)} %param.6) | copy-start | bytes 3000004
Sparse Core Ops, SparseCore 0:
  9.2 78.3 all-gather.4
  112.4 121.4 all-gather.6
  274.5 120.1 reduce-scatter.1
where the time goes:
time: 405 us; the launch traced here: 404 us
  waiting for transfers between devices  183 us (45%)
  local copies, waits for them, and re-layouts  102 us (25%)
  blocking collectives  74.8 us (18%)
  matrix products  27.8 us (7%)
  between operations  13.8 us (3%)
    reduce_scatter x1, waiting for transfers between devices, shards(): lax.psum_scatter(2.0 * coulomb_part - exchange_part, 'grp', scatter_dimen...  120 us
    unnamed x15, local copies, waits for them, and re-layouts  72.4 us
    all_gather x1, waiting for transfers between devices, shards(): lax.all_gather(orbitals, 'dev', axis=0, tiled=True)  61.7 us
    psum x1, blocking collectives, shards(): group_density = lax.psum(aux_density, 'dev')  54.1 us
    unnamed x1, blocking collectives  20.7 us
    slice x1, local copies, waits for them, and re-layouts, shards(): slab[aux_index].astype(jnp.float32)  17.1 us
    dot_general x1, matrix products, shards(): lax.dot_general(half_flat, lax.all_gather(half_flat, 'dev', axis=0, tiled...  15.5 us
    dot_general x1, matrix products, shards(): jnp.dot(slab_flat, lax.all_gather(orbitals, 'dev', axis=0, tiled=True), p...  12.2 us
  transfers between devices with their start and end apart: 3, of which 2 were waited for; matrix products, arithmetic and copies ran while one was open for 18% of the time, Pallas kernels for 0%

commit v1 on v0

--- a/solution.py
+++ b/solution.py
@@ -5,16 +5,19 @@
 
 
 def shards(slab, orbitals, hcore, metric_inv):
+
+    def review_keys(array_here, dim_at=0):
+        r_now = jnp.stack(lax.axis_size("dev") * [array_here])
+        new = lax.all_to_all(r_now, "dev", 0, 0)
+        kept_arr = jnp.concatenate(new, dim_at)
+        return kept_arr
+
     aux_count = slab.shape[0]
     row_count = slab.shape[1]
     full_width = slab.shape[2]
     occ_count = orbitals.shape[1]
     slab_flat = slab.reshape(aux_count * row_count, full_width)
-    half_done = jnp.dot(
-        slab_flat,
-        lax.all_gather(orbitals, "dev", axis=0, tiled=True),
-        preferred_element_type=jnp.float32,
-    )
+    half_done = jnp.dot(slab_flat, review_keys(orbitals), preferred_element_type=jnp.float32)
     half_done = half_done.astype(jnp.bfloat16).reshape(aux_count, row_count, occ_count)
     aux_density = jnp.sum(
         half_done.astype(jnp.float32) * orbitals.astype(jnp.float32)[None], axis=(1, 2)

time: 405 us -> 572 us (1.41)
  waiting for transfers between devices: 183 us -> 332 us
  starting transfers between devices: 0.08 us -> 11.3 us
    all_to_all x0 -> x1, waiting for transfers between devices: none -> 214 us  [review_keys(): new = lax.all_to_all(r_now, 'dev', 0, 0)]
    all_gather x1 -> x0, waiting for transfers between devices: 61.7 us -> none  [shards(): lax.all_gather(orbitals, 'dev', axis=0, tiled=True)]
    all_to_all x0 -> x1, starting transfers between devices: none -> 11.2 us  [review_keys(): new = lax.all_to_all(r_now, 'dev', 0, 0)]
    unnamed x15 -> x16, local copies, waits for them, and re-layouts: 72.4 us -> 61.3 us
    reshape x0 -> x1, local copies, waits for them, and re-layouts: none -> 10.9 us  [review_keys(): kept_arr = jnp.concatenate(new, dim_at)]
    another operation x0 -> x1, local copies, waits for them, and re-layouts: none -> 6.23 us  [review_keys(): r_now = jnp.stack(lax.axis_size('dev') * [array_here])]
  transfers between devices with their start and end apart: 3 -> 3, of which waited for: 2 -> 2; matrix products, arithmetic and copies ran while one was open for 18% -> 12% of each run, Pallas kernels for 0% -> 0%
where the time goes in v1:
time: 572 us; the launch traced here: 570 us
  waiting for transfers between devices  332 us (58%)
  local copies, waits for them, and re-layouts  107 us (19%)
  blocking collectives  75.1 us (13%)
  matrix products  27.8 us (5%)
  between operations  14.1 us (2%)
  starting transfers between devices  11.3 us (2%)
    all_to_all x1, waiting for transfers between devices, review_keys(): new = lax.all_to_all(r_now, 'dev', 0, 0)  214 us
    reduce_scatter x1, waiting for transfers between devices, shards(): lax.psum_scatter(2.0 * coulomb_part - exchange_part, 'grp', scatter_dimen...  119 us
    unnamed x16, local copies, waits for them, and re-layouts  61.3 us
    psum x1, blocking collectives, shards(): group_density = lax.psum(aux_density, 'dev')  54.6 us
    unnamed x1, blocking collectives  20.5 us
    slice x1, local copies, waits for them, and re-layouts, shards(): slab[aux_index].astype(jnp.float32)  17.1 us
    dot_general x1, matrix products, shards(): lax.dot_general(half_flat, lax.all_gather(half_flat, 'dev', axis=0, tiled...  15.5 us
    dot_general x1, matrix products, shards(): jnp.dot(slab_flat, review_keys(orbitals), preferred_element_type=jnp.floa...  12.2 us
  transfers between devices with their start and end apart: 3, of which 2 were waited for; matrix products, arithmetic and copies ran while one was open for 12% of the time, Pallas kernels for 0%

profile of v1, /device:TPU:1, one launch (start us, length us, event | category | flops | bytes accessed | tf_op | source)
XLA Modules:
  0.0 570.2 jit_solution(920191631142687440)
XLA Ops:
  6.5 6.2 %stack.2 = bf16[32,250,640]{2,1,0:T(8,128)(2,1)} broadcast(bf16[250,640]{1,0:T(8,128)(2,1)} %param.5), dimensions={1,2} | broadcast | bytes 10560000 | tf_op jit(solution)/shard_map/stack | solution.py:10
  12.8 11.2 %all-to-all-start = ((bf16[32,250,640]{2,1,0:T(8,128)(2,1)}), bf16[32,250,640]{2,1,0:T(8,128)(2,1)}, u32[]{:S(2)}, u32[]{:S(2)}) async-start(bf16[32,250,640]{2,1,0:T(8,128)(2,1)} %stack.2), calls=%async_computation | async-start | bytes 20971520 | tf_op jit(solution)/shard_map/all_to_all | solution.py:11
  24.0 0.0 all-gather.3.cloned.1.call-start
  24.1 0.1 mul.37
  24.2 0.1 mul.38
  24.3 7.3 %copy.19 = bf16[2,250,8000]{2,1,0:T(8,128)(2,1)} copy(bf16[2,250,8000]{2,0,1:T(2,128)(2,1)} %param.4) | data formatting | bytes 16000000 | tf_op args[0]
  31.6 10.0 %reshape.26 = bf16[500,8000]{1,0:T(8,128)(2,1)} reshape(bf16[2,250,8000]{2,1,0:T(8,128)(2,1)} %copy.19) | data formatting | bytes 16000000 | tf_op jit(solution)/shard_map/reshape | solution.py:19
  41.6 213.8 %all-to-all-done = bf16[32,250,640]{2,1,0:T(8,128)(2,1)} async-done(((bf16[32,250,640]{2,1,0:T(8,128)(2,1)}), bf16[32,250,640]{2,1,0:T(8,128)(2,1)}, u32[]{:S(2)}, u32[]{:S(2)}) %all-to-all-start) | async-done | bytes 10240032 | tf_op jit(solution)/shard_map/all_to_all | solution.py:11
  255.4 10.9 %reshape.27 = bf16[8000,640]{1,0:T(8,128)(2,1)} reshape(bf16[32,250,640]{2,1,0:T(8,128)(2,1)} %all-to-all-done) | data formatting | bytes 20480000 | tf_op jit(solution)/shard_map/reshape | solution.py:12
  266.4 12.2 %multiply_reduce_fusion = (f32[500]{0:T(512)S(1)}, bf16[500,640]{1,0:T(8,128)(2,1)S(1)}) fusion(f32[500,640]{1,0:T(8,128)S(1)} %mul.38, bf16[500,8000]{1,0:T(8,128)(2,1)} %reshape.26, bf16[8000,640]{1,0:T(8,128)(2,1)} %reshape.27), kind=kOutput, calls=%fused_computation.2 | convolution fusion | flops 5121279488 | bytes 20162000 | tf_op jit(solution)/shard_map/dot_general | solution.py:20
  278.6 0.1 reshape.28
  278.7 0.3 copy.22
  279.0 1.1 copy.24
  280.1 0.0 all-gather.3.cloned.1.call-update
  280.1 0.0 reduce-scatter.2.cloned.1.call-start
  280.1 17.1 %fusion.1 = (bf16[1,250,8000]{2,0,1:T(2,128)(2,1)}, bf16[1,250,8000]{2,0,1:T(2,128)(2,1)}) fusion(bf16[2,250,8000]{2,0,1:T(2,128)(2,1)} %param.4), kind=kLoop, calls=%fused_computation.5 | loop fusion | bytes 16000000 | tf_op jit(solution)/shard_map/slice | solution.py:39
  297.3 17.3 %copy.25 = bf16[1,250,8000]{1,2,0:T(8,128)(2,1)} copy(bf16[1,250,8000]{2,0,1:T(2,128)(2,1)} %get-tuple-element.5) | data formatting | bytes 8000000
  314.6 17.3 %copy.26 = bf16[1,250,8000]{1,2,0:T(8,128)(2,1)} copy(bf16[1,250,8000]{2,0,1:T(2,128)(2,1)} %get-tuple-element.6) | data formatting | bytes 8000000
  331.9 0.6 dynamic-slice.1
  332.5 0.1 reduce_sum.14
  332.6 0.1 reduce_sum.18
  333.3 54.6 %psum.7 = f32[2]{0:T(128)S(1)} all-reduce(f32[2]{0:T(128)S(1)} %reduce_sum.18), channel_id=1, replica_groups=mesh['grp'=8,'dev'=32] {'dev'}, use_global_device_ids=true, to_apply=%region_2.0 | all-reduce | flops 2 | bytes 16 | tf_op jit(solution)/shard_map/psum | solution.py:26
  387.9 0.2 dynamic-update-slice
  388.1 20.5 %all-reduce = f32[16]{0:T(128)S(1)} all-reduce(f32[16]{0:T(128)S(1)} %dynamic-update-slice), channel_id=1, replica_groups=mesh['grp'=8,'dev'=32] {'grp'}, use_global_device_ids=true, to_apply=%add | all-reduce | flops 16 | bytes 128
  408.6 0.1 convolution_bitcast_fusion
  408.7 0.1 dynamic_slice.3
  408.8 0.6 fusion.2
  409.4 17.5 %reshape.34 = bf16[8000,1280]{1,0:T(8,128)(2,1)} reshape(bf16[32,250,1280]{2,1,0:T(8,128)(2,1)} %all-gather.3.cloned.1.call-done) | data formatting | bytes 40960000
  426.9 15.5 %convolution_subtract_fusion = f32[250,8000]{0,1:T(8,128)} fusion(bf16[250,1280]{0,1:T(8,128)(2,1)S(1)} %bitcast.19, bf16[8000,1280]{1,0:T(8,128)(2,1)} %reshape.34, bf16[1,250,8000]{1,2,0:T(8,128)(2,1)} %copy.26, bf16[1,250,8000]{1,2,0:T(8,128)(2,1)} %copy.25, f32[]{:T(128)} %bitcast.4, f32[]{:T(128)} %bitcast.3), kind=kOutput, calls=%fused_computation | convolution fusion | flops 5134000128 | bytes 37120008 | tf_op jit(solution)/shard_map/dot_general | solution.py:30
  442.4 0.0 reduce-scatter.2.cloned.1.call-update
  442.4 118.6 %reduce-scatter.2.cloned.1.call-done = f32[250,1000]{0,1:T(8,128)} async-done(((f32[250,8000]{0,1:T(8,128)}), f32[250,1000]{0,1:T(8,128)}) %reduce-scatter.2.cloned.1.call-update) | async-done | bytes 1000016 | tf_op jit(solution)/shard_map/reduce_scatter | solution.py:40
  561.0 2.4 add.16
  (10 shorter events, 0.0 us)
Async XLA Ops:
  6.5 402.1 %copy-start = (f32[16,16]{1,0:T(8,128)S(1)}, f32[16,16]{1,0:T(8,128)}, u32[]{:S(2)}) copy-start(f32[16,16]{1,0:T(8,128)} %param.7) | copy-start | bytes 3076
  12.8 11.3 %copy-start.1 = (bf16[250,640]{1,0:T(8,128)(2,1)S(1)}, bf16[250,640]{1,0:T(8,128)(2,1)}, u32[]{:S(2)}) copy-start(bf16[250,640]{1,0:T(8,128)(2,1)} %param.5) | copy-start | bytes 960004
  12.8 242.7 %all-to-all-start = ((bf16[32,250,640]{2,1,0:T(8,128)(2,1)}), bf16[32,250,640]{2,1,0:T(8,128)(2,1)}, u32[]{:S(2)}, u32[]{:S(2)}) async-start(bf16[32,250,640]{2,1,0:T(8,128)(2,1)} %stack.2), calls=%async_computation | async-start | bytes 20971520 | tf_op jit(solution)/shard_map/all_to_all | solution.py:11
  24.0 385.4 %all-gather.3.cloned.1.call-start = ((), (), s32[]{:S(2)}) async-start(), calls=%async_computation.3 | async-start | bytes 21626880 | tf_op jit(solution)/shard_map/all_gather | solution.py:32
  280.1 280.9 %reduce-scatter.2.cloned.1.call-start = ((), (), s32[]{:S(2)}) async-start(), calls=%async_computation.2 | async-start | bytes 9216000 | tf_op jit(solution)/shard_map/reduce_scatter | solution.py:40
  314.6 17.3 %copy-start.3 = (u32[256]{0:T(256)S(1)}, u32[256]{0:T(256)}, u32[]{:S(2)}) copy-start(u32[256]{0:T(256)} %constant.21) | copy-start | bytes 3076
  442.4 118.6 %copy-start.2 = (f32[250,1000]{0,1:T(8,128)S(1)}, f32[250,1000]{0,1:T(8,128)}, u32[]{:S(2)}) copy-start(f32[250,1000]{0,1:T(8,128)} %param.6) | copy-start | bytes 3000004
Sparse Core Ops, SparseCore 0:
  280.2 119.0 all-gather.2
  442.6 118.3 reduce-scatter.1
